TPU v7x, 256 devices: a whole 4x4x8 slice. The times are simulated.
256 devices in a mesh: dp: 4 (over y), expert: 64 (over z, x, core).
Axes of the slice: x: 4, y: 4, z: 8, core: 2. Of those that a mesh axis runs over, the one named last changes fastest.
Arguments:
- hidden_states: bfloat16 [1024, 4, 4096], P('expert'), may hold values from -6 to 6
- routes: int32 [1024, 4, 8], P('expert'), may hold values from 0 to 63, all different within a row; in each aligned block of 64 rows (0 to 63, 64 to 127, ..., all dimensions but the last counted through in order) at most 16 rows name the same one
- route_weight: float32 [1024, 4, 8], P('expert'), may hold values from 0.05 to 1
- finish_step: int32 [1024], P('expert'), may hold values from 1 to 4
- group_keep: int32 [64], P('expert'), may hold values from 0 to 1
- dest_slot: int32 [1024], P('expert'), may hold values from 0 to 1023, as said below
- w_gate: bfloat16 [64, 4096, 1536], P('expert', None, 'dp'), may hold values from -0.09375 to 0.09375
- w_up: bfloat16 [64, 4096, 1536], P('expert', None, 'dp'), may hold values from -0.09375 to 0.09375
- w_down: bfloat16 [64, 1536, 4096], P('expert', 'dp'), may hold values from -0.15625 to 0.15625
Outputs:
- trainer_rows: bfloat16 [1024, 4, 4096], P(('dp', 'expert'))
Inputs may be any that keep to these rules, and one draw needn't show every extreme that they name: `routes`: in the 64 row-steps of one prompt group (rows g * 16 to (g + 1) * 16 - 1, all steps), no expert is named more than 16 times, a bound that some block reaches; a row names 8 different experts at each step. dest_slot is a permutation of the slots; row r of group g = r // 16 goes to a slot (d * 64 + g) * 4 + i with 0 <= d < 4 and 0 <= i < 4.
All inputs are finite; a program needn't handle non-finite values.
Results may differ from a plain program's by a relative error of at most 0.0049.
Values may be sent and summed in bfloat16 or wider, within the bound.
No kernel may reach another device: no remote copies, remote signals or barrier semaphores. Data moves between devices by JAX's collectives and lax.ppermute only.
A program may use at most 128 MiB of HBM per device.

v0:
```python
import jax
import jax.numpy as jnp
from jax import lax
from jax.sharding import PartitionSpec as P

MOST_BASE = 16


def exchange_gather(matrix, replica, replica_count):
    width = matrix.shape[1] // replica_count
    pieces = [lax.dynamic_slice_in_dim(matrix, replica * width, width, axis=1)]
    for shift in range(1, replica_count):
        start = (replica + shift) % replica_count * width
        outgoing = lax.dynamic_slice_in_dim(matrix, start, width, axis=1)
        pairs = [(i, (i + shift) % replica_count) for i in range(replica_count)]
        pieces.append(lax.ppermute(outgoing, "dp", pairs))
    return pieces


def exchange_all(block, replica_count):
    pieces = [block]
    for shift in range(1, replica_count):
        pairs = [(i, (i + shift) % replica_count) for i in range(replica_count)]
        pieces.append(lax.ppermute(block, "dp", pairs))
    return jnp.stack(pieces, axis=0)


def body(
    hidden_states, routes, route_weight, finish_step, group_keep, dest_slot, w_gate, w_up, w_down
):
    expert_count = lax.axis_size("expert")
    replica_count = lax.axis_size("dp")
    replica = lax.axis_index("dp")
    row_count, step_count, model_width = hidden_states.shape
    top_count = routes.shape[2]
    hidden_part = w_down.shape[1]
    columns = model_width // replica_count
    tokens = row_count * step_count
    slot_count = min(tokens, max(MOST_BASE, 2 * tokens * top_count // expert_count))
    slot_count = -(-slot_count // replica_count) * replica_count
    part = slot_count // replica_count
    down_cols = exchange_gather(w_down[0], replica, replica_count)
    step_ids = lax.broadcasted_iota(jnp.int32, (row_count, step_count), 1)
    live_mask = ((step_ids < finish_step[:, None]) & (group_keep[0] == 1)).reshape(tokens)
    gate_share = route_weight / jnp.sum(route_weight, axis=2, keepdims=True)
    expert_ids = lax.broadcasted_iota(jnp.int32, (1, 1, expert_count), 2)
    picked = (routes.reshape(tokens, top_count, 1) == expert_ids) & live_mask[:, None, None]
    hit_mask = jnp.sum(picked.astype(jnp.int32), axis=1)
    share_wide = jnp.broadcast_to(gate_share.reshape(tokens, top_count, 1), picked.shape)
    weight = jnp.sum(jnp.where(picked, share_wide, jnp.zeros_like(share_wide)), axis=1)
    prior_hits = jnp.cumsum(hit_mask, axis=0) - hit_mask
    flat_inputs = hidden_states.reshape(tokens, model_width)
    chunks = 2 if part % 2 == 0 else 1
    sub = part // chunks
    member_ids = lax.broadcasted_iota(jnp.int32, (1, 1, replica_count, 1), 2)
    within_ids = lax.broadcasted_iota(jnp.int32, (1, 1, 1, sub), 3)
    combined = jnp.zeros((tokens, columns), jnp.float32)
    outgoings = []
    for chunk in range(chunks):
        slot_ids = replica * part + chunk * sub + lax.broadcasted_iota(jnp.int32, (1, 1, sub), 2)
        placement = (hit_mask[:, :, None] == 1) & (prior_hits[:, :, None] == slot_ids)
        placement = placement.reshape(tokens, expert_count * sub)
        outgoings.append(
            lax.dot_general(
                placement.astype(jnp.bfloat16),
                flat_inputs,
                (((0,), (0,)), ((), ())),
                preferred_element_type=jnp.float32,
            ).astype(jnp.bfloat16)
        )
    if chunks > 1:
        down_cols, outgoings[1] = lax.optimization_barrier((down_cols, outgoings[1]))
    down_stack = jnp.stack(down_cols, axis=0)
    for chunk in range(chunks):
        outgoing = outgoings[chunk]
        arrived = lax.all_to_all(outgoing, "expert", split_axis=0, concat_axis=0, tiled=True)
        gathered = lax.all_gather(arrived, "dp", axis=0, tiled=True)
        gate_part = jnp.dot(gathered, w_gate[0], preferred_element_type=jnp.float32)
        up_part = jnp.dot(gathered, w_up[0], preferred_element_type=jnp.float32)
        activated = (jax.nn.silu(gate_part) * up_part).astype(jnp.bfloat16)
        hidden_all = exchange_all(activated, replica_count)
        expert_cols = lax.dot_general(
            hidden_all, down_stack, (((0, 2), (0, 1)), ((), ())), preferred_element_type=jnp.float32
        ).astype(jnp.bfloat16)
        by_source = expert_cols.reshape(replica_count, expert_count, sub, columns).transpose(
            1, 0, 2, 3
        )
        returned_rows = lax.all_to_all(by_source, "expert", split_axis=0, concat_axis=0, tiled=True)
        all_slot_ids = member_ids * part + chunk * sub + within_ids
        weighted_place = jnp.where(
            (hit_mask[:, :, None, None] == 1) & (prior_hits[:, :, None, None] == all_slot_ids),
            weight[:, :, None, None],
            0.0,
        ).reshape(tokens, expert_count * replica_count * sub)
        combined = combined + jnp.dot(
            weighted_place,
            returned_rows.reshape(expert_count * replica_count * sub, columns).astype(jnp.float32),
            precision=lax.Precision.HIGH,
            preferred_element_type=jnp.float32,
        )
    share_rows = row_count // replica_count
    flat_device = dest_slot // share_rows
    target = flat_device // expert_count * share_rows + dest_slot % share_rows
    position_ids = lax.broadcasted_iota(jnp.int32, (replica_count * share_rows, row_count), 0)
    arrangement = (target[None, :] == position_ids).astype(jnp.bfloat16)
    arranged = jnp.dot(
        arrangement,
        combined.astype(jnp.bfloat16).reshape(row_count, step_count * columns),
        preferred_element_type=jnp.float32,
    ).astype(jnp.bfloat16)
    arranged = arranged.reshape(replica_count, share_rows, step_count, columns)
    quarters = lax.all_to_all(arranged, "dp", split_axis=0, concat_axis=0, tiled=True)
    return quarters.transpose(1, 2, 0, 3).reshape(share_rows, step_count, model_width)


def solution(mesh):
    in_specs = (
        P("expert", None, None),
        P("expert", None, None),
        P("expert", None, None),
        P("expert"),
        P("expert"),
        P("expert"),
        P("expert", None, "dp"),
        P("expert", None, "dp"),
        P("expert", "dp", None),
    )
    out_specs = P(("dp", "expert"), None, None)
    return jax.shard_map(body, mesh=mesh, in_specs=in_specs, out_specs=out_specs, check_vma=False)
```

profile of v0, /device:TPU:2, one launch (start us, length us, event | category | flops | bytes accessed | tf_op | source)
XLA Modules:
  0.0 302.3 jit_solution(9261390843322471953)
XLA Ops:
  6.5 3.7 %dynamic-slice_bitcast_fusion = (bf16[384,1024]{1,0:T(8,128)(2,1)}, bf16[384,1024]{1,0:T(8,128)(2,1)}, bf16[384,1024]{1,0:T(8,128)(2,1)}, bf16[384,1024]{1,0:T(8,128)(2,1)}) fusion(bf16[1,384,4096]{2,1,0:T(8,128)(2,1)} %param.17, s32[]{:T(128)S(6)} %select_n.63, s32[]{:T(128)S(6)} %select_n.59, s32[]{:T(128)S(6)} %select_n.57, s32[]{:T(128)S(6)} %select_n.61), kind=kLoop, calls=%fused_computation.40 | loop fusion | bytes 6291472 | tf_op jit(solution)/shard_map/dynamic_slice | solution.py:14
  10.3 1.6 collective-permute-start.3
  11.9 2.9 collective-permute-start.4
  14.8 1.3 collective-permute-start.5
  16.1 0.1 copy.29
  16.9 0.1 fusion.55
  16.9 0.1 and.102
  17.0 0.2 convert_reduce_fusion
  17.3 0.1 reduce_window_sum.11
  17.4 0.1 copy.31
  17.5 0.1 copy.32
  17.6 0.2 compare_and_fusion.1
  17.8 2.0 reshape.213
  19.7 2.4 convolution_convert_fusion
  22.2 9.0 %collective-permute-done.3 = bf16[384,1024]{1,0:T(8,128)(2,1)} collective-permute-done((bf16[384,1024]{1,0:T(8,128)(2,1)}, bf16[384,1024]{1,0:T(8,128)(2,1)}, u32[]{:S(2)}, u32[]{:S(2)}) %collective-permute-start.3) | collective-permute-done | bytes 786464 | tf_op jit(solution)/shard_map/ppermute | solution.py:16
  31.2 18.0 %collective-permute-done.4 = bf16[384,1024]{1,0:T(8,128)(2,1)} collective-permute-done((bf16[384,1024]{1,0:T(8,128)(2,1)}, bf16[384,1024]{1,0:T(8,128)(2,1)}, u32[]{:S(2)}, u32[]{:S(2)}) %collective-permute-start.4) | collective-permute-done | bytes 786464 | tf_op jit(solution)/shard_map/ppermute | solution.py:16
  49.2 2.5 all_to_all.29
  51.7 40.9 %all_to_all.39 = bf16[64,2,4096]{2,1,0:T(2,128)(2,1)} all-to-all(bf16[64,2,4096]{2,1,0:T(2,128)(2,1)} %all_to_all.29), channel_id=1, replica_groups=mesh['dp'=4,'expert'=64] {'expert'}, dimensions={0} | all-to-all | bytes 2097152 | tf_op jit(solution)/shard_map/all_to_all | solution.py:76
  92.7 2.3 all_to_all.31
  95.0 0.0 all-gather.5.cloned.1.call-update
  95.0 0.0 all-gather.3.cloned.1.call-start
  95.1 2.4 convolution_convert_fusion.1
  97.5 2.5 all_to_all.25
  100.1 34.6 %all_to_all.40 = bf16[64,2,4096]{2,1,0:T(2,128)(2,1)} all-to-all(bf16[64,2,4096]{2,1,0:T(2,128)(2,1)} %all_to_all.25), channel_id=1, replica_groups=mesh['dp'=4,'expert'=64] {'expert'}, dimensions={0} | all-to-all | bytes 2097152 | tf_op jit(solution)/shard_map/all_to_all | solution.py:76
  134.6 2.3 all_to_all.27
  136.9 0.0 all-gather.3.cloned.1.call-update
  136.9 5.0 %all-gather.5.cloned.1.call-done = bf16[512,4096]{1,0:T(8,128)(2,1)} async-done(((bf16[128,4096]{1,0:T(8,128)(2,1)}), bf16[512,4096]{1,0:T(8,128)(2,1)}) %all-gather.5.cloned.1.call-update) | async-done | bytes 4194320 | tf_op jit(solution)/shard_map/all_gather | solution.py:77
  142.0 4.7 %fusion.4 = f32[512,384]{1,0:T(8,128)S(1)} fusion(bf16[512,4096]{1,0:T(8,128)(2,1)} %all-gather.5.cloned.1.call-done, bf16[1,4096,384]{2,1,0:T(8,128)(2,1)S(1)} %copy-done), kind=kOutput, calls=%fused_computation.8 | convolution fusion | flops 1610612736 | bytes 8126464 | tf_op jit(solution)/shard_map/dot_general | solution.py:78
  146.7 2.3 fusion.28
  149.0 1.2 collective-permute-start.8
  150.2 1.8 collective-permute-start.7
  152.0 0.6 collective-permute-start.6
  152.6 9.2 %collective-permute-done.8 = bf16[512,384]{1,0:T(8,128)(2,1)S(1)} collective-permute-done((bf16[512,384]{1,0:T(8,128)(2,1)S(1)}, bf16[512,384]{1,0:T(8,128)(2,1)S(1)}, u32[]{:S(2)}, u32[]{:S(2)}) %collective-permute-start.8) | collective-permute-done | bytes 393248 | tf_op jit(solution)/shard_map/ppermute | solution.py:24
  161.8 4.5 %collective-permute-done.7 = bf16[512,384]{1,0:T(8,128)(2,1)S(1)} collective-permute-done((bf16[512,384]{1,0:T(8,128)(2,1)S(1)}, bf16[512,384]{1,0:T(8,128)(2,1)S(1)}, u32[]{:S(2)}, u32[]{:S(2)}) %collective-permute-start.7) | collective-permute-done | bytes 393248 | tf_op jit(solution)/shard_map/ppermute | solution.py:24
  166.3 14.4 %collective-permute-done.6 = bf16[512,384]{1,0:T(8,128)(2,1)S(1)} collective-permute-done((bf16[512,384]{1,0:T(8,128)(2,1)S(1)}, bf16[512,384]{1,0:T(8,128)(2,1)S(1)}, u32[]{:S(2)}, u32[]{:S(2)}) %collective-permute-start.6) | collective-permute-done | bytes 393248 | tf_op jit(solution)/shard_map/ppermute | solution.py:24
  180.7 4.5 %bitcast_convert_fusion = bf16[512,1024]{1,0:T(8,128)(2,1)} fusion(bf16[1,512,384]{2,1,0:T(8,128)(2,1)S(1)} %bitcast.91, bf16[1,512,384]{2,1,0:T(8,128)(2,1)S(1)} %bitcast.93, bf16[1,512,384]{2,1,0:T(8,128)(2,1)S(1)} %bitcast.94, bf16[1,512,384]{2,1,0:T(8,128)(2,1)S(1)} %bitcast.88, bf16[1,384,1024]{2,1,0:T(8,128)(2,1)} %bitcast.16, ...), kind=kOutput, calls=%fused_computation.12 | convolution fusion | flops 1618214912 | bytes 5767168 | tf_op jit(solution)/shard_map/dot_general | solution.py:82
  185.2 2.2 reshape.215
  187.5 3.4 %copy.47 = bf16[4,64,2,1024]{3,2,0,1:T(2,128)(2,1)} copy(bf16[4,64,2,1024]{3,2,1,0:T(2,128)(2,1)} %reshape.215) | data formatting | bytes 2097152 | tf_op jit(solution)/shard_map/reshape | solution.py:85
  190.8 10.7 %all-to-all-start.3 = ((bf16[64,4,2,1024]{3,2,1,0:T(2,128)(2,1)}), bf16[64,4,2,1024]{3,2,1,0:T(2,128)(2,1)}, u32[]{:S(2)}, u32[]{:S(2)}) async-start(bf16[64,4,2,1024]{3,2,1,0:T(2,128)(2,1)} %bitcast.79), calls=%async_computation.3 | async-start | bytes 2097152 | tf_op jit(solution)/shard_map/all_to_all | solution.py:88
  201.6 3.2 %all-gather.3.cloned.1.call-done = bf16[512,4096]{1,0:T(8,128)(2,1)} async-done(((bf16[128,4096]{1,0:T(8,128)(2,1)}), bf16[512,4096]{1,0:T(8,128)(2,1)}) %all-gather.3.cloned.1.call-update) | async-done | bytes 4194320 | tf_op jit(solution)/shard_map/all_gather | solution.py:77
  204.8 4.7 %fusion.6 = f32[512,384]{1,0:T(8,128)S(1)} fusion(bf16[512,4096]{1,0:T(8,128)(2,1)} %all-gather.3.cloned.1.call-done, bf16[1,4096,384]{2,1,0:T(8,128)(2,1)S(1)} %copy-done), kind=kOutput, calls=%fused_computation.10 | convolution fusion | flops 1610612736 | bytes 8126464 | tf_op jit(solution)/shard_map/dot_general | solution.py:78
  209.5 2.3 fusion.31
  211.8 0.7 collective-permute-start.2
  212.5 1.8 collective-permute-start.1
  214.3 0.8 collective-permute-start
  215.1 8.8 %collective-permute-done.2 = bf16[512,384]{1,0:T(8,128)(2,1)S(1)} collective-permute-done((bf16[512,384]{1,0:T(8,128)(2,1)S(1)}, bf16[512,384]{1,0:T(8,128)(2,1)S(1)}, u32[]{:S(2)}, u32[]{:S(2)}) %collective-permute-start.2) | collective-permute-done | bytes 393248 | tf_op jit(solution)/shard_map/ppermute | solution.py:24
  223.9 2.2 collective-permute-done.1
  226.1 7.2 %collective-permute-done = bf16[512,384]{1,0:T(8,128)(2,1)S(1)} collective-permute-done((bf16[512,384]{1,0:T(8,128)(2,1)S(1)}, bf16[512,384]{1,0:T(8,128)(2,1)S(1)}, u32[]{:S(2)}, u32[]{:S(2)}) %collective-permute-start) | collective-permute-done | bytes 393248 | tf_op jit(solution)/shard_map/ppermute | solution.py:24
  233.3 4.4 %bitcast_convert_fusion.1 = bf16[512,1024]{1,0:T(8,128)(2,1)} fusion(bf16[1,512,384]{2,1,0:T(8,128)(2,1)S(1)} %bitcast.89, bf16[1,512,384]{2,1,0:T(8,128)(2,1)S(1)} %bitcast.90, bf16[1,512,384]{2,1,0:T(8,128)(2,1)S(1)} %bitcast.92, bf16[1,512,384]{2,1,0:T(8,128)(2,1)S(1)} %bitcast.87, bf16[1,384,1024]{2,1,0:T(8,128)(2,1)} %bitcast.16, ...), kind=kOutput, calls=%fused_computation.13 | convolution fusion | flops 1618214912 | bytes 5767168 | tf_op jit(solution)/shard_map/dot_general | solution.py:82
  237.7 2.3 reshape.214
  239.9 3.4 %copy.48 = bf16[4,64,2,1024]{3,2,0,1:T(2,128)(2,1)} copy(bf16[4,64,2,1024]{3,2,1,0:T(2,128)(2,1)} %reshape.214) | data formatting | bytes 2097152 | tf_op jit(solution)/shard_map/reshape | solution.py:85
  243.3 10.7 %all-to-all-start.1 = ((bf16[64,4,2,1024]{3,2,1,0:T(2,128)(2,1)}), bf16[64,4,2,1024]{3,2,1,0:T(2,128)(2,1)}, u32[]{:S(2)}, u32[]{:S(2)}) async-start(bf16[64,4,2,1024]{3,2,1,0:T(2,128)(2,1)} %bitcast.80), calls=%async_computation.1 | async-start | bytes 2097152 | tf_op jit(solution)/shard_map/all_to_all | solution.py:88
  254.1 0.1 copy.30
  254.2 0.3 select_reduce_fusion
  254.5 0.1 iota_add_fusion
  254.6 0.1 iota_add_fusion.1
  254.7 3.5 %convolution_bitcast_fusion = f32[64,1024]{1,0:T(8,128)} fusion(bf16[64,4,2,1024]{3,2,1,0:T(2,128)(2,1)} %all-to-all-done.3, s32[4,2]{1,0:T(4,128)S(1)} %iota_add_fusion, f32[64,64]{1,0:T(8,128)S(1)} %select_reduce_fusion, s32[64,64]{1,0:T(8,128)S(1)} %sub.20, pred[64,64]{1,0:T(8,128)(4,1)S(1)} %broadcast_compare_fusion), kind=kOutput, calls=%fused_computation.32 | convolution fusion | flops 201424896 | bytes 1347616 | tf_op jit(solution)/shard_map/dot_general | solution.py:95
  258.2 24.6 %all-to-all-done.1 = bf16[64,4,2,1024]{3,2,1,0:T(2,128)(2,1)} async-done(((bf16[64,4,2,1024]{3,2,1,0:T(2,128)(2,1)}), bf16[64,4,2,1024]{3,2,1,0:T(2,128)(2,1)}, u32[]{:S(2)}, u32[]{:S(2)}) %all-to-all-start.1) | async-done | bytes 1048608 | tf_op jit(solution)/shard_map/all_to_all | solution.py:88
  282.8 2.8 fusion.35
  285.6 0.1 reshape.216
  285.7 0.2 convolution_convert_fusion.2
  285.9 0.1 reshape.217
  285.9 8.8 %all_to_all.41 = bf16[4,4,4,1024]{3,2,1,0:T(4,128)(2,1)S(1)} all-to-all(bf16[4,4,4,1024]{3,2,1,0:T(4,128)(2,1)S(1)} %reshape.217), channel_id=1, replica_groups=mesh['dp'=4,'expert'=64] {'dp'}, dimensions={0} | all-to-all | bytes 262144 | tf_op jit(solution)/shard_map/all_to_all | solution.py:112
  294.7 0.7 copy.40
  (35 shorter events, 0.2 us)
Async XLA Ops:
  6.5 135.4 %copy-start = (bf16[1,4096,384]{2,1,0:T(8,128)(2,1)S(1)}, bf16[1,4096,384]{2,1,0:T(8,128)(2,1)}, u32[]{:S(2)}) copy-start(bf16[1,4096,384]{2,1,0:T(8,128)(2,1)} %param.15) | copy-start | bytes 9437188
  6.5 135.4 %all-gather.5.cloned.1.call-start = ((), (), s32[]{:S(2)}) async-start(), calls=%async_computation.6 | async-start | bytes 5242880 | tf_op jit(solution)/shard_map/all_gather | solution.py:77
  6.5 9.6 %copy-start.4 = (s32[16,4,8]{0,2,1:T(8,128)S(1)}, s32[16,4,8]{0,2,1:T(8,128)}, u32[]{:S(2)}) copy-start(s32[16,4,8]{0,2,1:T(8,128)} %param.10) | copy-start | bytes 6148
  6.5 10.3 %copy-start.5 = (s32[16]{0:T(128)S(1)}, s32[16]{0:T(128)}, u32[]{:S(2)}) copy-start(s32[16]{0:T(128)} %param.12) | copy-start | bytes 196
  10.3 20.9 %collective-permute-start.3 = (bf16[384,1024]{1,0:T(8,128)(2,1)}, bf16[384,1024]{1,0:T(8,128)(2,1)}, u32[]{:S(2)}, u32[]{:S(2)}) collective-permute-start(bf16[384,1024]{1,0:T(8,128)(2,1)} %get-tuple-element.16), channel_id=1, source_target_pairs={{0,64},{64,128},{128,192},{192,0},{1,65},{65,129},{129,193},{193,1... | collective-permute-start | bytes 2359304 | tf_op jit(solution)/shard_map/ppermute | solution.py:16
  11.9 37.3 %collective-permute-start.4 = (bf16[384,1024]{1,0:T(8,128)(2,1)}, bf16[384,1024]{1,0:T(8,128)(2,1)}, u32[]{:S(2)}, u32[]{:S(2)}) collective-permute-start(bf16[384,1024]{1,0:T(8,128)(2,1)} %get-tuple-element.18), channel_id=1, source_target_pairs={{0,128},{64,192},{128,0},{192,64},{1,129},{65,193},{129,1},{193,65... | collective-permute-start | bytes 2359304 | tf_op jit(solution)/shard_map/ppermute | solution.py:16
  14.8 34.4 %collective-permute-start.5 = (bf16[384,1024]{1,0:T(8,128)(2,1)}, bf16[384,1024]{1,0:T(8,128)(2,1)}, u32[]{:S(2)}, u32[]{:S(2)}) collective-permute-start(bf16[384,1024]{1,0:T(8,128)(2,1)} %get-tuple-element.15), channel_id=1, source_target_pairs={{0,192},{64,0},{128,64},{192,128},{1,193},{65,1},{129,65},{193,129... | collective-permute-start | bytes 2359304 | tf_op jit(solution)/shard_map/ppermute | solution.py:16
  95.0 109.8 %all-gather.3.cloned.1.call-start = ((), (), s32[]{:S(2)}) async-start(), calls=%async_computation.5 | async-start | bytes 5242880 | tf_op jit(solution)/shard_map/all_gather | solution.py:77
  142.0 4.7 %copy-start.7 = (bf16[512,4096]{1,0:T(8,128)(2,1)S(1)}, bf16[512,4096]{1,0:T(8,128)(2,1)}, u32[]{:S(2)}) copy-start(bf16[512,4096]{1,0:T(8,128)(2,1)} %all-gather.5.cloned.1.call-done) | copy-start | bytes 12582916
  142.0 4.7 %copy-start.8 = (bf16[1,4096,384]{2,1,0:T(8,128)(2,1)S(1)}, bf16[1,4096,384]{2,1,0:T(8,128)(2,1)}, u32[]{:S(2)}) copy-start(bf16[1,4096,384]{2,1,0:T(8,128)(2,1)} %param.16) | copy-start | bytes 9437188
  146.6 34.1 %copy-start.1 = (bf16[384,1024]{1,0:T(8,128)(2,1)S(1)}, bf16[384,1024]{1,0:T(8,128)(2,1)}, u32[]{:S(2)}) copy-start(bf16[384,1024]{1,0:T(8,128)(2,1)} %get-tuple-element.10) | copy-start | bytes 2359300
  149.0 12.8 %collective-permute-start.8 = (bf16[512,384]{1,0:T(8,128)(2,1)S(1)}, bf16[512,384]{1,0:T(8,128)(2,1)S(1)}, u32[]{:S(2)}, u32[]{:S(2)}) collective-permute-start(bf16[512,384]{1,0:T(8,128)(2,1)S(1)} %fusion.28), channel_id=1, source_target_pairs={{0,192},{64,0},{128,64},{192,128},{1,193},{65,1},{129,65},{193,129... | collective-permute-start | bytes 1179656 | tf_op jit(solution)/shard_map/ppermute | solution.py:24
  150.2 16.1 %collective-permute-start.7 = (bf16[512,384]{1,0:T(8,128)(2,1)S(1)}, bf16[512,384]{1,0:T(8,128)(2,1)S(1)}, u32[]{:S(2)}, u32[]{:S(2)}) collective-permute-start(bf16[512,384]{1,0:T(8,128)(2,1)S(1)} %fusion.28), channel_id=1, source_target_pairs={{0,128},{64,192},{128,0},{192,64},{1,129},{65,193},{129,1},{193,65... | collective-permute-start | bytes 1179656 | tf_op jit(solution)/shard_map/ppermute | solution.py:24
  152.0 28.7 %collective-permute-start.6 = (bf16[512,384]{1,0:T(8,128)(2,1)S(1)}, bf16[512,384]{1,0:T(8,128)(2,1)S(1)}, u32[]{:S(2)}, u32[]{:S(2)}) collective-permute-start(bf16[512,384]{1,0:T(8,128)(2,1)S(1)} %fusion.28), channel_id=1, source_target_pairs={{0,64},{64,128},{128,192},{192,0},{1,65},{65,129},{129,193},{193,1... | collective-permute-start | bytes 1179656 | tf_op jit(solution)/shard_map/ppermute | solution.py:24
  190.8 52.5 %all-to-all-start.3 = ((bf16[64,4,2,1024]{3,2,1,0:T(2,128)(2,1)}), bf16[64,4,2,1024]{3,2,1,0:T(2,128)(2,1)}, u32[]{:S(2)}, u32[]{:S(2)}) async-start(bf16[64,4,2,1024]{3,2,1,0:T(2,128)(2,1)} %bitcast.79), calls=%async_computation.3 | async-start | bytes 2097152 | tf_op jit(solution)/shard_map/all_to_all | solution.py:88
  204.8 4.7 %copy-start.6 = (bf16[512,4096]{1,0:T(8,128)(2,1)S(1)}, bf16[512,4096]{1,0:T(8,128)(2,1)}, u32[]{:S(2)}) copy-start(bf16[512,4096]{1,0:T(8,128)(2,1)} %all-gather.3.cloned.1.call-done) | copy-start | bytes 12582916
  204.8 4.7 %copy-start.9 = (bf16[1,4096,384]{2,1,0:T(8,128)(2,1)S(1)}, bf16[1,4096,384]{2,1,0:T(8,128)(2,1)}, u32[]{:S(2)}) copy-start(bf16[1,4096,384]{2,1,0:T(8,128)(2,1)} %param.16) | copy-start | bytes 9437188
  209.5 23.8 %copy-start.2 = (bf16[384,1024]{1,0:T(8,128)(2,1)S(1)}, bf16[384,1024]{1,0:T(8,128)(2,1)}, u32[]{:S(2)}) copy-start(bf16[384,1024]{1,0:T(8,128)(2,1)} %get-tuple-element.10) | copy-start | bytes 2359300
  211.8 12.0 %collective-permute-start.2 = (bf16[512,384]{1,0:T(8,128)(2,1)S(1)}, bf16[512,384]{1,0:T(8,128)(2,1)S(1)}, u32[]{:S(2)}, u32[]{:S(2)}) collective-permute-start(bf16[512,384]{1,0:T(8,128)(2,1)S(1)} %fusion.31), channel_id=1, source_target_pairs={{0,192},{64,0},{128,64},{192,128},{1,193},{65,1},{129,65},{193,129... | collective-permute-start | bytes 1179656 | tf_op jit(solution)/shard_map/ppermute | solution.py:24
  212.5 13.6 %collective-permute-start.1 = (bf16[512,384]{1,0:T(8,128)(2,1)S(1)}, bf16[512,384]{1,0:T(8,128)(2,1)S(1)}, u32[]{:S(2)}, u32[]{:S(2)}) collective-permute-start(bf16[512,384]{1,0:T(8,128)(2,1)S(1)} %fusion.31), channel_id=1, source_target_pairs={{0,128},{64,192},{128,0},{192,64},{1,129},{65,193},{129,1},{193,65... | collective-permute-start | bytes 1179656 | tf_op jit(solution)/shard_map/ppermute | solution.py:24
  214.3 18.9 %collective-permute-start = (bf16[512,384]{1,0:T(8,128)(2,1)S(1)}, bf16[512,384]{1,0:T(8,128)(2,1)S(1)}, u32[]{:S(2)}, u32[]{:S(2)}) collective-permute-start(bf16[512,384]{1,0:T(8,128)(2,1)S(1)} %fusion.31), channel_id=1, source_target_pairs={{0,64},{64,128},{128,192},{192,0},{1,65},{65,129},{129,193},{193,1... | collective-permute-start | bytes 1179656 | tf_op jit(solution)/shard_map/ppermute | solution.py:24
  237.7 16.4 %copy-start.3 = (f32[16,4,8]{0,2,1:T(8,128)S(1)}, f32[16,4,8]{0,2,1:T(8,128)}, u32[]{:S(2)}) copy-start(f32[16,4,8]{0,2,1:T(8,128)} %param.11) | copy-start | bytes 6148
  237.7 16.8 %copy-start.10 = (s32[16]{0:T(128)S(1)}, s32[16]{0:T(128)}, u32[]{:S(2)}) copy-start(s32[16]{0:T(128)} %param.14) | copy-start | bytes 196
  243.3 39.5 %all-to-all-start.1 = ((bf16[64,4,2,1024]{3,2,1,0:T(2,128)(2,1)}), bf16[64,4,2,1024]{3,2,1,0:T(2,128)(2,1)}, u32[]{:S(2)}, u32[]{:S(2)}) async-start(bf16[64,4,2,1024]{3,2,1,0:T(2,128)(2,1)} %bitcast.80), calls=%async_computation.1 | async-start | bytes 2097152 | tf_op jit(solution)/shard_map/all_to_all | solution.py:88
Sparse Core Ops, SparseCore 0:
  95.1 46.8 all-gather.4
  143.8 60.9 all-gather.2
where the time goes:
time: 303 us; the launch traced here: 302 us
  waiting for transfers between devices  106 us (35%)
  blocking collectives  84.3 us (28%)
  matrix products  34.3 us (11%)
  starting transfers between devices  34.2 us (11%)
  local copies, waits for them, and re-layouts  28 us (9%)
  between operations  14.3 us (5%)
    all_to_all x2, blocking collectives, body(): lax.all_to_all(outgoing, 'expert', split_axis=0, concat_axis=0, tiled=True)  75.5 us
    ppermute x6, waiting for transfers between devices, exchange_all(): pieces.append(lax.ppermute(block, 'dp', pairs))  46.3 us
    ppermute x3, waiting for transfers between devices, exchange_gather(): pieces.append(lax.ppermute(outgoing, 'dp', pairs))  27 us
    all_to_all x2, waiting for transfers between devices, body(): lax.all_to_all(by_source, 'expert', split_axis=0, concat_axis=0, tiled=True)  24.6 us
    all_to_all x2, starting transfers between devices, body(): lax.all_to_all(by_source, 'expert', split_axis=0, concat_axis=0, tiled=True)  21.5 us
    reshape x4, local copies, waits for them, and re-layouts, body(): expert_cols.reshape(replica_count, expert_count, sub, columns)  11.2 us
    all_to_all x4, local copies, waits for them, and re-layouts, body(): lax.all_to_all(outgoing, 'expert', split_axis=0, concat_axis=0, tiled=True)  9.66 us
    dot_general x2, matrix products, body(): gate_part = jnp.dot(gathered, w_gate[0], preferred_element_type=jnp.float32)  9.32 us
  transfers between devices with their start and end apart: 13, of which 11 were waited for; matrix products, arithmetic and copies ran while one was open for 15% of the time, Pallas kernels for 0%

commit v1 on v0

--- a/solution.py
+++ b/solution.py
@@ -74,7 +74,25 @@
     for chunk in range(chunks):
         outgoing = outgoings[chunk]
         arrived = lax.all_to_all(outgoing, "expert", split_axis=0, concat_axis=0, tiled=True)
-        gathered = lax.all_gather(arrived, "dp", axis=0, tiled=True)
+        ways, here, lap = (lax.axis_size("dp"), lax.axis_index("dp"), arrived.shape[0])
+        lengths = [n * ways if d == 0 else n for d, n in enumerate(arrived.shape)]
+        full = lax.dynamic_update_slice_in_dim(
+            jnp.zeros(lengths, arrived.dtype), arrived, here * lap, axis=0
+        )
+        going_up = going_down = arrived
+        for far in range(1, ways // 2 + 1):
+            going_up = lax.ppermute(going_up, "dp", [(d, (d + 1) % ways) for d in range(ways)])
+            full = lax.dynamic_update_slice_in_dim(
+                full, going_up, (here - far) % ways * lap, axis=0
+            )
+            if 2 * far < ways:
+                going_down = lax.ppermute(
+                    going_down, "dp", [(d, (d - 1) % ways) for d in range(ways)]
+                )
+                full = lax.dynamic_update_slice_in_dim(
+                    full, going_down, (here + far) % ways * lap, axis=0
+                )
+        gathered = full
         gate_part = jnp.dot(gathered, w_gate[0], preferred_element_type=jnp.float32)
         up_part = jnp.dot(gathered, w_up[0], preferred_element_type=jnp.float32)
         activated = (jax.nn.silu(gate_part) * up_part).astype(jnp.bfloat16)

time: 303 us -> 316 us (1.043)
  blocking collectives: 84.3 us -> 8.36 us
  waiting for transfers between devices: 106 us -> 171 us
  starting transfers between devices: 34.2 us -> 59.2 us
  between operations: 14.3 us -> 1.02 us
  local copies, waits for them, and re-layouts: 28 us -> 38.8 us
    all_to_all x2 -> x0, blocking collectives: 75.5 us -> none  [body(): lax.all_to_all(outgoing, 'expert', split_axis=0, concat_axis=0, tiled=True)]
    ppermute x0 -> x6, waiting for transfers between devices: none -> 58 us  [the longest x4 58 us: body(): lax.ppermute(going_up, 'dp', [(d, (d + 1) % ways) for d in range(ways)])]
    all_to_all x0 -> x2, waiting for transfers between devices: none -> 23.2 us  [body(): lax.all_to_all(outgoing, 'expert', split_axis=0, concat_axis=0, tiled=True)]
    all_to_all x0 -> x2, starting transfers between devices: none -> 22.7 us  [body(): lax.all_to_all(outgoing, 'expert', split_axis=0, concat_axis=0, tiled=True)]
    ppermute x6, waiting for transfers between devices: 46.3 us -> 34.6 us  [exchange_all(): pieces.append(lax.ppermute(block, 'dp', pairs))]
    all_gather x2 -> x0, waiting for transfers between devices: 8.25 us -> none  [body(): gathered = lax.all_gather(arrived, 'dp', axis=0, tiled=True)]
    dynamic_update_slice x0 -> x8, local copies, waits for them, and re-layouts: none -> 7.13 us  [the longest x4 3.56 us: body(): lax.dynamic_update_slice_in_dim(full, going_up, (here - far) % ways * lap...]
    ppermute x0 -> x6, starting transfers between devices: none -> 6.53 us  [the longest x2 4.16 us: body(): lax.ppermute(going_down, 'dp', [(d, (d - 1) % ways) for d in range(ways)])]
  transfers between devices with their start and end apart: 13 -> 19, of which waited for: 11 -> 12; matrix products, arithmetic and copies ran while one was open for 15% -> 14% of each run, Pallas kernels for 0% -> 0%
where the time goes in v1:
time: 316 us; the launch traced here: 315 us
  waiting for transfers between devices  171 us (54%)
  starting transfers between devices  59.2 us (19%)
  local copies, waits for them, and re-layouts  38.8 us (12%)
  matrix products  34.2 us (11%)
  blocking collectives  8.36 us (3%)
    ppermute x4, waiting for transfers between devices, body(): lax.ppermute(going_up, 'dp', [(d, (d + 1) % ways) for d in range(ways)])  58 us
    ppermute x6, waiting for transfers between devices, exchange_all(): pieces.append(lax.ppermute(block, 'dp', pairs))  34.6 us
    ppermute x3, waiting for transfers between devices, exchange_gather(): pieces.append(lax.ppermute(outgoing, 'dp', pairs))  30.9 us
    all_to_all x2, waiting for transfers between devices, body(): lax.all_to_all(by_source, 'expert', split_axis=0, concat_axis=0, tiled=True)  24.6 us
    all_to_all x2, waiting for transfers between devices, body(): lax.all_to_all(outgoing, 'expert', split_axis=0, concat_axis=0, tiled=True)  23.2 us
    all_to_all x2, starting transfers between devices, body(): lax.all_to_all(outgoing, 'expert', split_axis=0, concat_axis=0, tiled=True)  22.7 us
    all_to_all x2, starting transfers between devices, body(): lax.all_to_all(by_source, 'expert', split_axis=0, concat_axis=0, tiled=True)  18.8 us
    reshape x4, local copies, waits for them, and re-layouts, body(): expert_cols.reshape(replica_count, expert_count, sub, columns)  11.3 us
  transfers between devices with their start and end apart: 19, of which 12 were waited for; matrix products, arithmetic and copies ran while one was open for 14% of the time, Pallas kernels for 0%

profile of v1, /device:TPU:2, one launch (start us, length us, event | category | flops | bytes accessed | tf_op | source)
XLA Modules:
  0.0 314.7 jit_solution(17874820144742846507)
XLA Ops:
  0.0 0.9 copy.29
  1.6 0.7 fusion.43
  2.4 0.2 convert_reduce_fusion
  3.0 2.0 reshape.213
  5.0 0.2 compare_and_fusion.1
  5.2 2.5 convolution_convert_fusion.1
  7.6 2.5 all_to_all.25
  10.2 12.2 %all-to-all-start = ((bf16[64,2,4096]{2,1,0:T(2,128)(2,1)}), bf16[64,2,4096]{2,1,0:T(2,128)(2,1)}, u32[]{:S(2)}, u32[]{:S(2)}) async-start(bf16[64,2,4096]{2,1,0:T(2,128)(2,1)} %all_to_all.25), calls=%async_computation | async-start | bytes 2097152 | tf_op jit(solution)/shard_map/all_to_all | solution.py:76
  22.4 3.6 %dynamic-slice_bitcast_fusion = (bf16[384,1024]{1,0:T(8,128)(2,1)}, bf16[384,1024]{1,0:T(8,128)(2,1)}, bf16[384,1024]{1,0:T(8,128)(2,1)}, bf16[384,1024]{1,0:T(8,128)(2,1)}) fusion(bf16[1,384,4096]{2,1,0:T(8,128)(2,1)} %param.17, s32[]{:T(128)S(6)} %select_n.101, s32[]{:T(128)S(6)} %select_n.97, s32[]{:T(128)S(6)} %select_n.96, s32[]{:T(128)S(6)} %select_n.99), kind=kLoop, calls=%fused_computation.37 | loop fusion | bytes 6291472 | tf_op jit(solution)/shard_map/dynamic_slice | solution.py:14
  26.0 1.6 collective-permute-start.6
  27.6 2.9 collective-permute-start.7
  30.5 1.3 collective-permute-start.8
  31.9 2.4 convolution_convert_fusion
  34.3 12.9 %collective-permute-done.6 = bf16[384,1024]{1,0:T(8,128)(2,1)} collective-permute-done((bf16[384,1024]{1,0:T(8,128)(2,1)}, bf16[384,1024]{1,0:T(8,128)(2,1)}, u32[]{:S(2)}, u32[]{:S(2)}) %collective-permute-start.6) | collective-permute-done | bytes 786464 | tf_op jit(solution)/shard_map/ppermute | solution.py:16
  47.2 18.0 %collective-permute-done.7 = bf16[384,1024]{1,0:T(8,128)(2,1)} collective-permute-done((bf16[384,1024]{1,0:T(8,128)(2,1)}, bf16[384,1024]{1,0:T(8,128)(2,1)}, u32[]{:S(2)}, u32[]{:S(2)}) %collective-permute-start.7) | collective-permute-done | bytes 786464 | tf_op jit(solution)/shard_map/ppermute | solution.py:16
  65.3 2.5 all_to_all.29
  67.8 10.5 %all-to-all-start.2 = ((bf16[64,2,4096]{2,1,0:T(2,128)(2,1)}), bf16[64,2,4096]{2,1,0:T(2,128)(2,1)}, u32[]{:S(2)}, u32[]{:S(2)}) async-start(bf16[64,2,4096]{2,1,0:T(2,128)(2,1)} %all_to_all.29), calls=%async_computation.2 | async-start | bytes 2097152 | tf_op jit(solution)/shard_map/all_to_all | solution.py:76
  78.3 2.3 all_to_all.27
  80.5 1.1 collective-permute-start
  81.7 2.1 collective-permute-start.1
  83.8 23.2 %all-to-all-done.2 = bf16[64,2,4096]{2,1,0:T(2,128)(2,1)} async-done(((bf16[64,2,4096]{2,1,0:T(2,128)(2,1)}), bf16[64,2,4096]{2,1,0:T(2,128)(2,1)}, u32[]{:S(2)}, u32[]{:S(2)}) %all-to-all-start.2) | async-done | bytes 1048608 | tf_op jit(solution)/shard_map/all_to_all | solution.py:76
  107.0 2.3 all_to_all.31
  109.3 1.1 collective-permute-start.9
  110.4 2.4 broadcast.189.clone.1
  112.9 1.1 constant_dynamic-update-slice_fusion.7
  113.9 2.1 collective-permute-start.10
  116.0 0.5 broadcast.189.clone
  116.5 0.1 constant_dynamic-update-slice_fusion.3
  116.7 2.3 constant_dynamic-update-slice_fusion.6
  119.0 17.8 %collective-permute-done.9 = bf16[128,4096]{1,0:T(8,128)(2,1)S(1)} collective-permute-done((bf16[128,4096]{1,0:T(8,128)(2,1)}, bf16[128,4096]{1,0:T(8,128)(2,1)S(1)}, u32[]{:S(2)}, u32[]{:S(2)}) %collective-permute-start.9) | collective-permute-done | bytes 1048608 | tf_op jit(solution)/shard_map/ppermute | solution.py:84
  136.8 2.3 constant_dynamic-update-slice_fusion.5
  139.3 40.2 %collective-permute-done.11 = bf16[128,4096]{1,0:T(8,128)(2,1)S(1)} collective-permute-done((bf16[128,4096]{1,0:T(8,128)(2,1)S(1)}, bf16[128,4096]{1,0:T(8,128)(2,1)S(1)}, u32[]{:S(2)}, u32[]{:S(2)}) %collective-permute-start.11) | collective-permute-done | bytes 1048608 | tf_op jit(solution)/shard_map/ppermute | solution.py:84
  179.7 2.3 fusion.4
  182.0 2.3 multiply_convert_fusion
  184.4 0.9 collective-permute-start.14
  185.3 1.1 collective-permute-start.13
  186.5 0.8 collective-permute-start.12
  187.3 1.0 constant_dynamic-update-slice_fusion.4
  188.3 8.2 %collective-permute-done.14 = bf16[512,384]{1,0:T(8,128)(2,1)S(1)} collective-permute-done((bf16[512,384]{1,0:T(8,128)(2,1)S(1)}, bf16[512,384]{1,0:T(8,128)(2,1)S(1)}, u32[]{:S(2)}, u32[]{:S(2)}) %collective-permute-start.14) | collective-permute-done | bytes 393248 | tf_op jit(solution)/shard_map/ppermute | solution.py:24
  196.5 2.4 collective-permute-done.13
  198.9 5.0 %collective-permute-done.12 = bf16[512,384]{1,0:T(8,128)(2,1)S(1)} collective-permute-done((bf16[512,384]{1,0:T(8,128)(2,1)S(1)}, bf16[512,384]{1,0:T(8,128)(2,1)S(1)}, u32[]{:S(2)}, u32[]{:S(2)}) %collective-permute-start.12) | collective-permute-done | bytes 393248 | tf_op jit(solution)/shard_map/ppermute | solution.py:24
  203.9 4.4 %bitcast_convert_fusion = bf16[512,1024]{1,0:T(8,128)(2,1)} fusion(bf16[1,512,384]{2,1,0:T(8,128)(2,1)S(1)} %bitcast.85, bf16[1,512,384]{2,1,0:T(8,128)(2,1)S(1)} %bitcast.86, bf16[1,512,384]{2,1,0:T(8,128)(2,1)S(1)} %bitcast.88, bf16[1,512,384]{2,1,0:T(8,128)(2,1)S(1)} %bitcast.83, bf16[1,384,1024]{2,1,0:T(8,128)(2,1)} %bitcast.16, ...), kind=kOutput, calls=%fused_computation.12 | convolution fusion | flops 1618214912 | bytes 5767168 | tf_op jit(solution)/shard_map/dot_general | solution.py:100
  208.4 2.2 reshape.215
  210.6 3.4 %copy.47 = bf16[4,64,2,1024]{3,2,0,1:T(2,128)(2,1)} copy(bf16[4,64,2,1024]{3,2,1,0:T(2,128)(2,1)} %reshape.215) | data formatting | bytes 2097152 | tf_op jit(solution)/shard_map/reshape | solution.py:103
  214.0 8.3 %all-to-all-start.3 = ((bf16[64,4,2,1024]{3,2,1,0:T(2,128)(2,1)}), bf16[64,4,2,1024]{3,2,1,0:T(2,128)(2,1)}, u32[]{:S(2)}, u32[]{:S(2)}) async-start(bf16[64,4,2,1024]{3,2,1,0:T(2,128)(2,1)} %bitcast.75), calls=%async_computation.3 | async-start | bytes 2097152 | tf_op jit(solution)/shard_map/all_to_all | solution.py:106
  222.3 4.7 %fusion.6 = f32[512,384]{1,0:T(8,128)S(1)} fusion(bf16[512,4096]{1,0:T(8,128)(2,1)} %constant_dynamic-update-slice_fusion.4, bf16[1,4096,384]{2,1,0:T(8,128)(2,1)S(1)} %copy-done), kind=kOutput, calls=%fused_computation.10 | convolution fusion | flops 1610612736 | bytes 8126464 | tf_op jit(solution)/shard_map/dot_general | solution.py:96
  227.0 4.6 %multiply_convert_fusion.1 = bf16[512,384]{1,0:T(8,128)(2,1)S(1)} fusion(f32[512,384]{1,0:T(8,128)S(1)} %fusion.6, bf16[512,4096]{1,0:T(8,128)(2,1)} %constant_dynamic-update-slice_fusion.4, bf16[1,4096,384]{2,1,0:T(8,128)(2,1)S(1)} %copy-done.7), kind=kOutput, calls=%fused_computation.41 | convolution fusion | flops 1611792384 | bytes 8519680 | tf_op jit(solution)/shard_map/dot_general | solution.py:97
  231.6 0.7 collective-permute-start.5
  232.3 1.0 collective-permute-start.4
  233.3 0.8 collective-permute-start.3
  234.1 9.5 %collective-permute-done.5 = bf16[512,384]{1,0:T(8,128)(2,1)S(1)} collective-permute-done((bf16[512,384]{1,0:T(8,128)(2,1)S(1)}, bf16[512,384]{1,0:T(8,128)(2,1)S(1)}, u32[]{:S(2)}, u32[]{:S(2)}) %collective-permute-start.5) | collective-permute-done | bytes 393248 | tf_op jit(solution)/shard_map/ppermute | solution.py:24
  243.7 2.2 collective-permute-done.4
  245.8 7.3 %collective-permute-done.3 = bf16[512,384]{1,0:T(8,128)(2,1)S(1)} collective-permute-done((bf16[512,384]{1,0:T(8,128)(2,1)S(1)}, bf16[512,384]{1,0:T(8,128)(2,1)S(1)}, u32[]{:S(2)}, u32[]{:S(2)}) %collective-permute-start.3) | collective-permute-done | bytes 393248 | tf_op jit(solution)/shard_map/ppermute | solution.py:24
  253.1 4.5 %bitcast_convert_fusion.1 = bf16[512,1024]{1,0:T(8,128)(2,1)} fusion(bf16[1,512,384]{2,1,0:T(8,128)(2,1)S(1)} %bitcast.87, bf16[1,512,384]{2,1,0:T(8,128)(2,1)S(1)} %bitcast.89, bf16[1,512,384]{2,1,0:T(8,128)(2,1)S(1)} %bitcast.90, bf16[1,512,384]{2,1,0:T(8,128)(2,1)S(1)} %bitcast.84, bf16[1,384,1024]{2,1,0:T(8,128)(2,1)} %bitcast.16, ...), kind=kOutput, calls=%fused_computation.13 | convolution fusion | flops 1618214912 | bytes 5767168 | tf_op jit(solution)/shard_map/dot_general | solution.py:100
  257.6 2.3 reshape.214
  259.9 3.4 %copy.48 = bf16[4,64,2,1024]{3,2,0,1:T(2,128)(2,1)} copy(bf16[4,64,2,1024]{3,2,1,0:T(2,128)(2,1)} %reshape.214) | data formatting | bytes 2097152 | tf_op jit(solution)/shard_map/reshape | solution.py:103
  263.2 10.5 %all-to-all-start.1 = ((bf16[64,4,2,1024]{3,2,1,0:T(2,128)(2,1)}), bf16[64,4,2,1024]{3,2,1,0:T(2,128)(2,1)}, u32[]{:S(2)}, u32[]{:S(2)}) async-start(bf16[64,4,2,1024]{3,2,1,0:T(2,128)(2,1)} %bitcast.76), calls=%async_computation.1 | async-start | bytes 2097152 | tf_op jit(solution)/shard_map/all_to_all | solution.py:106
  273.9 0.3 select_reduce_fusion
  274.3 3.5 %convolution_bitcast_fusion = f32[64,1024]{1,0:T(8,128)} fusion(bf16[64,4,2,1024]{3,2,1,0:T(2,128)(2,1)} %all-to-all-done.3, s32[4,2]{1,0:T(4,128)S(1)} %iota_add_fusion, f32[64,64]{1,0:T(8,128)S(1)} %select_reduce_fusion, s32[64,64]{1,0:T(8,128)S(1)} %sub.28, pred[64,64]{1,0:T(8,128)(4,1)S(1)} %broadcast_compare_fusion), kind=kOutput, calls=%fused_computation.28 | convolution fusion | flops 201424896 | bytes 1347616 | tf_op jit(solution)/shard_map/dot_general | solution.py:113
  277.8 24.6 %all-to-all-done.1 = bf16[64,4,2,1024]{3,2,1,0:T(2,128)(2,1)} async-done(((bf16[64,4,2,1024]{3,2,1,0:T(2,128)(2,1)}), bf16[64,4,2,1024]{3,2,1,0:T(2,128)(2,1)}, u32[]{:S(2)}, u32[]{:S(2)}) %all-to-all-start.1) | async-done | bytes 1048608 | tf_op jit(solution)/shard_map/all_to_all | solution.py:106
  302.4 2.8 fusion.23
  305.4 0.2 convolution_convert_fusion.2
  305.6 8.4 %all_to_all.39 = bf16[4,4,4,1024]{3,2,1,0:T(4,128)(2,1)S(1)} all-to-all(bf16[4,4,4,1024]{3,2,1,0:T(4,128)(2,1)S(1)} %reshape.217), channel_id=1, replica_groups=mesh['dp'=4,'expert'=64] {'dp'}, dimensions={0} | all-to-all | bytes 262144 | tf_op jit(solution)/shard_map/all_to_all | solution.py:130
  314.0 0.7 copy.40
  (49 shorter events, 1.4 us)
Async XLA Ops:
  0.0 179.7 %copy-start = (bf16[1,4096,384]{2,1,0:T(8,128)(2,1)S(1)}, bf16[1,4096,384]{2,1,0:T(8,128)(2,1)}, u32[]{:S(2)}) copy-start(bf16[1,4096,384]{2,1,0:T(8,128)(2,1)} %param.15) | copy-start | bytes 9437188
  10.2 57.6 %all-to-all-start = ((bf16[64,2,4096]{2,1,0:T(2,128)(2,1)}), bf16[64,2,4096]{2,1,0:T(2,128)(2,1)}, u32[]{:S(2)}, u32[]{:S(2)}) async-start(bf16[64,2,4096]{2,1,0:T(2,128)(2,1)} %all_to_all.25), calls=%async_computation | async-start | bytes 2097152 | tf_op jit(solution)/shard_map/all_to_all | solution.py:76
  26.0 21.2 %collective-permute-start.6 = (bf16[384,1024]{1,0:T(8,128)(2,1)}, bf16[384,1024]{1,0:T(8,128)(2,1)}, u32[]{:S(2)}, u32[]{:S(2)}) collective-permute-start(bf16[384,1024]{1,0:T(8,128)(2,1)} %get-tuple-element.16), channel_id=1, source_target_pairs={{0,64},{64,128},{128,192},{192,0},{1,65},{65,129},{129,193},{193,1... | collective-permute-start | bytes 2359304 | tf_op jit(solution)/shard_map/ppermute | solution.py:16
  27.6 37.6 %collective-permute-start.7 = (bf16[384,1024]{1,0:T(8,128)(2,1)}, bf16[384,1024]{1,0:T(8,128)(2,1)}, u32[]{:S(2)}, u32[]{:S(2)}) collective-permute-start(bf16[384,1024]{1,0:T(8,128)(2,1)} %get-tuple-element.18), channel_id=1, source_target_pairs={{0,128},{64,192},{128,0},{192,64},{1,129},{65,193},{129,1},{193,65... | collective-permute-start | bytes 2359304 | tf_op jit(solution)/shard_map/ppermute | solution.py:16
  30.5 34.7 %collective-permute-start.8 = (bf16[384,1024]{1,0:T(8,128)(2,1)}, bf16[384,1024]{1,0:T(8,128)(2,1)}, u32[]{:S(2)}, u32[]{:S(2)}) collective-permute-start(bf16[384,1024]{1,0:T(8,128)(2,1)} %get-tuple-element.15), channel_id=1, source_target_pairs={{0,192},{64,0},{128,64},{192,128},{1,193},{65,1},{129,65},{193,129... | collective-permute-start | bytes 2359304 | tf_op jit(solution)/shard_map/ppermute | solution.py:16
  67.8 39.2 %all-to-all-start.2 = ((bf16[64,2,4096]{2,1,0:T(2,128)(2,1)}), bf16[64,2,4096]{2,1,0:T(2,128)(2,1)}, u32[]{:S(2)}, u32[]{:S(2)}) async-start(bf16[64,2,4096]{2,1,0:T(2,128)(2,1)} %all_to_all.29), calls=%async_computation.2 | async-start | bytes 2097152 | tf_op jit(solution)/shard_map/all_to_all | solution.py:76
  80.5 36.1 %collective-permute-start = (bf16[128,4096]{1,0:T(8,128)(2,1)}, bf16[128,4096]{1,0:T(8,128)(2,1)}, u32[]{:S(2)}, u32[]{:S(2)}) collective-permute-start(bf16[128,4096]{1,0:T(8,128)(2,1)} %all_to_all.27), channel_id=1, source_target_pairs={{0,64},{64,128},{128,192},{192,0},{1,65},{65,129},{129,193},{193,1... | collective-permute-start | bytes 3145736 | tf_op jit(solution)/shard_map/ppermute | solution.py:84
  81.7 55.1 %collective-permute-start.1 = (bf16[128,4096]{1,0:T(8,128)(2,1)}, bf16[128,4096]{1,0:T(8,128)(2,1)}, u32[]{:S(2)}, u32[]{:S(2)}) collective-permute-start(bf16[128,4096]{1,0:T(8,128)(2,1)} %all_to_all.27), channel_id=1, source_target_pairs={{0,192},{64,0},{128,64},{192,128},{1,193},{65,1},{129,65},{193,129... | collective-permute-start | bytes 3145736 | tf_op jit(solution)/shard_map/ppermute | solution.py:89
  109.3 3.6 %copy-start.1 = (bf16[128,4096]{1,0:T(8,128)(2,1)S(1)}, bf16[128,4096]{1,0:T(8,128)(2,1)}, u32[]{:S(2)}) copy-start(bf16[128,4096]{1,0:T(8,128)(2,1)} %all_to_all.27) | copy-start | bytes 3145732
  109.3 4.7 %copy-start.2 = (bf16[128,4096]{1,0:T(8,128)(2,1)S(1)}, bf16[128,4096]{1,0:T(8,128)(2,1)}, u32[]{:S(2)}) copy-start(bf16[128,4096]{1,0:T(8,128)(2,1)} %all_to_all.31) | copy-start | bytes 3145732
  109.3 27.5 %collective-permute-start.9 = (bf16[128,4096]{1,0:T(8,128)(2,1)}, bf16[128,4096]{1,0:T(8,128)(2,1)S(1)}, u32[]{:S(2)}, u32[]{:S(2)}) collective-permute-start(bf16[128,4096]{1,0:T(8,128)(2,1)} %all_to_all.31), channel_id=1, source_target_pairs={{0,64},{64,128},{128,192},{192,0},{1,65},{65,129},{129,193},{193,1... | collective-permute-start | bytes 3145736 | tf_op jit(solution)/shard_map/ppermute | solution.py:84
  113.9 25.3 %collective-permute-start.10 = (bf16[128,4096]{1,0:T(8,128)(2,1)S(1)}, bf16[128,4096]{1,0:T(8,128)(2,1)S(1)}, u32[]{:S(2)}, u32[]{:S(2)}) collective-permute-start(bf16[128,4096]{1,0:T(8,128)(2,1)S(1)} %copy-done.2), channel_id=1, source_target_pairs={{0,192},{64,0},{128,64},{192,128},{1,193},{65,1},{129,65},{193,129... | collective-permute-start | bytes 3145736 | tf_op jit(solution)/shard_map/ppermute | solution.py:89
  116.6 70.6 %collective-permute-start.2 = (bf16[128,4096]{1,0:T(8,128)(2,1)}, bf16[128,4096]{1,0:T(8,128)(2,1)S(1)}, u32[]{:S(2)}, u32[]{:S(2)}) collective-permute-start(bf16[128,4096]{1,0:T(8,128)(2,1)} %collective-permute-done), channel_id=1, source_target_pairs={{0,64},{64,128},{128,192},{192,0},{1,65},{65,129},{129,193},{193,1... | collective-permute-start | bytes 3145736 | tf_op jit(solution)/shard_map/ppermute | solution.py:84
  136.8 42.8 %collective-permute-start.11 = (bf16[128,4096]{1,0:T(8,128)(2,1)S(1)}, bf16[128,4096]{1,0:T(8,128)(2,1)S(1)}, u32[]{:S(2)}, u32[]{:S(2)}) collective-permute-start(bf16[128,4096]{1,0:T(8,128)(2,1)S(1)} %collective-permute-done.9), channel_id=1, source_target_pairs={{0,64},{64,128},{128,192},{192,0},{1,65},{65,129},{129,193},{193,1... | collective-permute-start | bytes 3145736 | tf_op jit(solution)/shard_map/ppermute | solution.py:84
  179.7 2.3 copy-start.6
  182.0 21.9 %copy-start.3 = (bf16[384,1024]{1,0:T(8,128)(2,1)S(1)}, bf16[384,1024]{1,0:T(8,128)(2,1)}, u32[]{:S(2)}) copy-start(bf16[384,1024]{1,0:T(8,128)(2,1)} %get-tuple-element.10) | copy-start | bytes 2359300
  184.4 12.1 %collective-permute-start.14 = (bf16[512,384]{1,0:T(8,128)(2,1)S(1)}, bf16[512,384]{1,0:T(8,128)(2,1)S(1)}, u32[]{:S(2)}, u32[]{:S(2)}) collective-permute-start(bf16[512,384]{1,0:T(8,128)(2,1)S(1)} %multiply_convert_fusion), channel_id=1, source_target_pairs={{0,192},{64,0},{128,64},{192,128},{1,193},{65,1},{129,65},{193,129... | collective-permute-start | bytes 1179656 | tf_op jit(solution)/shard_map/ppermute | solution.py:24
  185.3 13.6 %collective-permute-start.13 = (bf16[512,384]{1,0:T(8,128)(2,1)S(1)}, bf16[512,384]{1,0:T(8,128)(2,1)S(1)}, u32[]{:S(2)}, u32[]{:S(2)}) collective-permute-start(bf16[512,384]{1,0:T(8,128)(2,1)S(1)} %multiply_convert_fusion), channel_id=1, source_target_pairs={{0,128},{64,192},{128,0},{192,64},{1,129},{65,193},{129,1},{193,65... | collective-permute-start | bytes 1179656 | tf_op jit(solution)/shard_map/ppermute | solution.py:24
  186.5 17.5 %collective-permute-start.12 = (bf16[512,384]{1,0:T(8,128)(2,1)S(1)}, bf16[512,384]{1,0:T(8,128)(2,1)S(1)}, u32[]{:S(2)}, u32[]{:S(2)}) collective-permute-start(bf16[512,384]{1,0:T(8,128)(2,1)S(1)} %multiply_convert_fusion), channel_id=1, source_target_pairs={{0,64},{64,128},{128,192},{192,0},{1,65},{65,129},{129,193},{193,1... | collective-permute-start | bytes 1179656 | tf_op jit(solution)/shard_map/ppermute | solution.py:24
  214.0 49.3 %all-to-all-start.3 = ((bf16[64,4,2,1024]{3,2,1,0:T(2,128)(2,1)}), bf16[64,4,2,1024]{3,2,1,0:T(2,128)(2,1)}, u32[]{:S(2)}, u32[]{:S(2)}) async-start(bf16[64,4,2,1024]{3,2,1,0:T(2,128)(2,1)} %bitcast.75), calls=%async_computation.3 | async-start | bytes 2097152 | tf_op jit(solution)/shard_map/all_to_all | solution.py:106
  222.3 4.7 %copy-start.7 = (bf16[1,4096,384]{2,1,0:T(8,128)(2,1)S(1)}, bf16[1,4096,384]{2,1,0:T(8,128)(2,1)}, u32[]{:S(2)}) copy-start(bf16[1,4096,384]{2,1,0:T(8,128)(2,1)} %param.16) | copy-start | bytes 9437188
  227.0 26.2 %copy-start.4 = (bf16[384,1024]{1,0:T(8,128)(2,1)S(1)}, bf16[384,1024]{1,0:T(8,128)(2,1)}, u32[]{:S(2)}) copy-start(bf16[384,1024]{1,0:T(8,128)(2,1)} %get-tuple-element.10) | copy-start | bytes 2359300
  231.6 12.0 %collective-permute-start.5 = (bf16[512,384]{1,0:T(8,128)(2,1)S(1)}, bf16[512,384]{1,0:T(8,128)(2,1)S(1)}, u32[]{:S(2)}, u32[]{:S(2)}) collective-permute-start(bf16[512,384]{1,0:T(8,128)(2,1)S(1)} %multiply_convert_fusion.1), channel_id=1, source_target_pairs={{0,192},{64,0},{128,64},{192,128},{1,193},{65,1},{129,65},{193,129... | collective-permute-start | bytes 1179656 | tf_op jit(solution)/shard_map/ppermute | solution.py:24
  232.3 13.5 %collective-permute-start.4 = (bf16[512,384]{1,0:T(8,128)(2,1)S(1)}, bf16[512,384]{1,0:T(8,128)(2,1)S(1)}, u32[]{:S(2)}, u32[]{:S(2)}) collective-permute-start(bf16[512,384]{1,0:T(8,128)(2,1)S(1)} %multiply_convert_fusion.1), channel_id=1, source_target_pairs={{0,128},{64,192},{128,0},{192,64},{1,129},{65,193},{129,1},{193,65... | collective-permute-start | bytes 1179656 | tf_op jit(solution)/shard_map/ppermute | solution.py:24
  233.3 19.8 %collective-permute-start.3 = (bf16[512,384]{1,0:T(8,128)(2,1)S(1)}, bf16[512,384]{1,0:T(8,128)(2,1)S(1)}, u32[]{:S(2)}, u32[]{:S(2)}) collective-permute-start(bf16[512,384]{1,0:T(8,128)(2,1)S(1)} %multiply_convert_fusion.1), channel_id=1, source_target_pairs={{0,64},{64,128},{128,192},{192,0},{1,65},{65,129},{129,193},{193,1... | collective-permute-start | bytes 1179656 | tf_op jit(solution)/shard_map/ppermute | solution.py:24
  257.6 16.2 %copy-start.5 = (f32[16,4,8]{0,2,1:T(8,128)S(1)}, f32[16,4,8]{0,2,1:T(8,128)}, u32[]{:S(2)}) copy-start(f32[16,4,8]{0,2,1:T(8,128)} %param.11) | copy-start | bytes 6148
  257.6 16.6 %copy-start.8 = (s32[16]{0:T(128)S(1)}, s32[16]{0:T(128)}, u32[]{:S(2)}) copy-start(s32[16]{0:T(128)} %param.14) | copy-start | bytes 196
  263.2 39.2 %all-to-all-start.1 = ((bf16[64,4,2,1024]{3,2,1,0:T(2,128)(2,1)}), bf16[64,4,2,1024]{3,2,1,0:T(2,128)(2,1)}, u32[]{:S(2)}, u32[]{:S(2)}) async-start(bf16[64,4,2,1024]{3,2,1,0:T(2,128)(2,1)} %bitcast.76), calls=%async_computation.1 | async-start | bytes 2097152 | tf_op jit(solution)/shard_map/all_to_all | solution.py:106
